TPU v7x, 512 devices: a whole 4x4x16 slice. The times are simulated.
512 devices in a mesh: blk: 16 (over x_hi, y, core), wide: 32 (over x_lo, z).
Axes of the slice: x: 4 (x_hi: 2, x_lo: 2; x = x_hi * 2 + x_lo), y: 4, z: 16, core: 2. Of those that a mesh axis runs over, the one named last changes fastest.
Arguments:
- series: bfloat16 [90112, 640], P(('blk', 'wide'))
- scrub_mask: int32 [640], replicated, may hold values from 0 to 1, as said below
- seed_index: int32 [4096], P(('blk', 'wide')), may hold values from 0 to 90111, as said below
Outputs:
- dispersion: bfloat16 [16, 5632, 4096], P(None, 'wide', 'blk')
- statistic: bfloat16 [16, 5632, 4096], P(None, 'wide', 'blk')
Inputs may be any that keep to these rules, and one draw needn't show every extreme that they name: Entry i of seed_index lies among the rows (i // 8) * 176 to (i // 8 + 1) * 176 - 1, and the 8 entries of one such block are distinct. `scrub_mask`: every frame of even position is kept.
All inputs are finite; a program needn't handle non-finite values.
Results may differ from a plain program's by a relative error of at most 0.0057.
Values may be sent and summed in bfloat16 or wider, within the bound.
No kernel may reach another device: no remote copies, remote signals or barrier semaphores. Data moves between devices by JAX's collectives and lax.ppermute only.
A program may use at most 128 MiB of HBM per device.

v0:
```python
import jax
import jax.numpy as jnp
from jax import lax
from jax.sharding import PartitionSpec as P

WIN = 60
STRIDE = 30
NWIN = 20
EPSILON = 1e-05
CLIP_LEVEL = 0.99


def shifted(block, axis, distance):
    devices = range(lax.axis_size(axis))
    route = [((i - distance) % len(devices), i) for i in devices]
    return lax.ppermute(block, axis, route)


def fisher_of(values):
    clipped = jnp.clip(values, -CLIP_LEVEL, CLIP_LEVEL)
    return 0.5 * (jnp.log(1.0 + clipped) - jnp.log(1.0 - clipped))


def prepare(raw_rows, scrub_mask):
    values = raw_rows.astype(jnp.float32)
    row_count = values.shape[0]
    weight = scrub_mask.astype(jnp.float32)
    covered = STRIDE * (NWIN + 1)
    pieces = values[:, :covered].reshape(row_count, NWIN + 1, STRIDE)
    framed = jnp.concatenate([pieces[:, :-1], pieces[:, 1:]], axis=2)
    mask_pieces = weight[:covered].reshape(NWIN + 1, STRIDE)
    mask_framed = jnp.concatenate([mask_pieces[:-1], mask_pieces[1:]], axis=1)
    valid_count = jnp.sum(mask_framed, axis=1)
    centre = jnp.sum(framed * mask_framed, axis=2) / valid_count
    centred = (framed - centre[:, :, None]) * mask_framed
    spread = jnp.sum(centred * centred, axis=2)
    windows = (centred * lax.rsqrt(spread + EPSILON)[:, :, None]).astype(jnp.bfloat16)
    total_valid = jnp.sum(weight)
    mean_all = jnp.sum(values * weight, axis=1) / total_valid
    centred_all = (values - mean_all[:, None]) * weight
    spread_all = jnp.sum(centred_all * centred_all, axis=1)
    whole_std = (centred_all * lax.rsqrt(spread_all + EPSILON)[:, None]).astype(jnp.bfloat16)
    return (windows, whole_std)


def compare(target_windows, target_whole, seed_window, seed_whole, total_valid):
    window_corr = jnp.einsum(
        "tnw,snw->nts", target_windows, seed_window, preferred_element_type=jnp.float32
    )
    fisher = fisher_of(window_corr)
    first_moment = jnp.mean(fisher, axis=0)
    second = jnp.mean(fisher * fisher, axis=0)
    dispersion = ((WIN - 3) * (second - first_moment * first_moment)).astype(jnp.bfloat16)
    static = jnp.einsum("tf,sf->ts", target_whole, seed_whole, preferred_element_type=jnp.float32)
    statistic = (jnp.sqrt(total_valid - 3.0) * fisher_of(static)).astype(jnp.bfloat16)
    return (dispersion, statistic)


def body(series, scrub_mask, seed_index):
    row_count = series.shape[0]
    local_rows = seed_index % row_count
    own_seeds = jnp.take(series, local_rows, axis=0)
    total_valid = jnp.sum(scrub_mask.astype(jnp.float32))
    target_windows, target_whole = prepare(series, scrub_mask)
    blocks = lax.axis_size("blk")
    panel_rows = lax.all_gather(own_seeds, "wide", axis=0, tiled=True)
    seed_window, seed_whole = prepare(panel_rows, scrub_mask)
    panel_size = panel_rows.shape[0]
    own_block = lax.axis_index("blk")

    def record(results, source, raw_rows):
        block_windows, block_whole = prepare(raw_rows, scrub_mask)
        dispersion, statistic = compare(
            block_windows, block_whole, seed_window, seed_whole, total_valid
        )
        return (
            lax.dynamic_update_index_in_dim(results[0], dispersion, source, 0),
            lax.dynamic_update_index_in_dim(results[1], statistic, source, 0),
        )

    empty = jnp.zeros((blocks, row_count, panel_size), jnp.bfloat16)
    own_dispersion, own_statistic = compare(
        target_windows, target_whole, seed_window, seed_whole, total_valid
    )
    results = (
        lax.dynamic_update_index_in_dim(empty, own_dispersion, own_block, 0),
        lax.dynamic_update_index_in_dim(empty, own_statistic, own_block, 0),
    )

    def advance(offset, carry):
        stored, moving = carry
        moving = shifted(moving, "blk", 1)
        stored = record(stored, (own_block - offset) % blocks, moving)
        return (stored, moving)

    results, moving = lax.fori_loop(1, blocks, advance, (results, series))
    return (results[0], results[1])


def solution(mesh):
    in_specs = (P(("blk", "wide"), None), P(), P(("blk", "wide")))
    out_specs = (P(None, "wide", "blk"), P(None, "wide", "blk"))
    return jax.shard_map(body, mesh=mesh, in_specs=in_specs, out_specs=out_specs, check_vma=False)
```

profile of v0, /device:TPU:4, one launch (start us, length us, event | category | flops | bytes accessed | tf_op | source)
XLA Modules:
  0.0 359.1 jit_solution(2068689304347063946)
XLA Ops:
  8.9 70.2 %all_gather.3 = bf16[256,640]{1,0:T(8,128)(2,1)S(1)} all-gather(bf16[8,640]{1,0:T(8,128)(2,1)S(1)} %broadcast_select_fusion), channel_id=1, replica_groups=mesh['blk'=16,'wide'=32] {'wide'}, dimensions={0}, use_global_device_ids=true | all-gather | bytes 337920 | tf_op jit(solution)/shard_map/all_gather | solution.py:66
  85.3 2.3 multiply_reduce_fusion.5
  90.4 267.5 %while.20 = (s32[]{:T(128)}, bf16[16,176,256]{2,1,0:T(8,128)(2,1)}, bf16[16,176,256]{2,1,0:T(8,128)(2,1)S(1)}, bf16[176,640]{0,1:T(8,128)(2,1)S(1)}, f32[20,60]{...) while((s32[]{:T(128)}, bf16[16,176,256]{2,1,0:T(8,128)(2,1)}, ...), condition=%wide.region_20.21_spmd, body=%wide.region_13.20_spmd.sunk | while | flops 177675536 | bytes 12591712 | solution.py:96
  92.4 10.0 %collective-permute-done = bf16[176,640]{0,1:T(8,128)(2,1)S(1)} collective-permute-done((bf16[176,640]{0,1:T(8,128)(2,1)S(1)}, bf16[176,640]{0,1:T(8,128)(2,1)S(1)}, u32[]{:S(2)}, u32[]{:S(2)}) %collective-permute-start) | collective-permute-done | bytes 225312 | tf_op jit(solution)/shard_map/while/body/eval_jaxpr/ppermute | solution.py:16
  110.2 10.0 %collective-permute-done = bf16[176,640]{0,1:T(8,128)(2,1)S(1)} collective-permute-done((bf16[176,640]{0,1:T(8,128)(2,1)S(1)}, bf16[176,640]{0,1:T(8,128)(2,1)S(1)}, u32[]{:S(2)}, u32[]{:S(2)}) %collective-permute-start) | collective-permute-done | bytes 225312 | tf_op jit(solution)/shard_map/while/body/eval_jaxpr/ppermute | solution.py:16
  122.6 2.3 multiply_reduce_fusion.21
  128.1 10.0 %collective-permute-done = bf16[176,640]{0,1:T(8,128)(2,1)S(1)} collective-permute-done((bf16[176,640]{0,1:T(8,128)(2,1)S(1)}, bf16[176,640]{0,1:T(8,128)(2,1)S(1)}, u32[]{:S(2)}, u32[]{:S(2)}) %collective-permute-start) | collective-permute-done | bytes 225312 | tf_op jit(solution)/shard_map/while/body/eval_jaxpr/ppermute | solution.py:16
  140.4 2.3 multiply_reduce_fusion.21
  145.9 10.0 %collective-permute-done = bf16[176,640]{0,1:T(8,128)(2,1)S(1)} collective-permute-done((bf16[176,640]{0,1:T(8,128)(2,1)S(1)}, bf16[176,640]{0,1:T(8,128)(2,1)S(1)}, u32[]{:S(2)}, u32[]{:S(2)}) %collective-permute-start) | collective-permute-done | bytes 225312 | tf_op jit(solution)/shard_map/while/body/eval_jaxpr/ppermute | solution.py:16
  158.2 2.3 multiply_reduce_fusion.21
  163.7 10.0 %collective-permute-done = bf16[176,640]{0,1:T(8,128)(2,1)S(1)} collective-permute-done((bf16[176,640]{0,1:T(8,128)(2,1)S(1)}, bf16[176,640]{0,1:T(8,128)(2,1)S(1)}, u32[]{:S(2)}, u32[]{:S(2)}) %collective-permute-start) | collective-permute-done | bytes 225312 | tf_op jit(solution)/shard_map/while/body/eval_jaxpr/ppermute | solution.py:16
  176.1 2.3 multiply_reduce_fusion.21
  181.6 10.0 %collective-permute-done = bf16[176,640]{0,1:T(8,128)(2,1)S(1)} collective-permute-done((bf16[176,640]{0,1:T(8,128)(2,1)S(1)}, bf16[176,640]{0,1:T(8,128)(2,1)S(1)}, u32[]{:S(2)}, u32[]{:S(2)}) %collective-permute-start) | collective-permute-done | bytes 225312 | tf_op jit(solution)/shard_map/while/body/eval_jaxpr/ppermute | solution.py:16
  193.9 2.3 multiply_reduce_fusion.21
  199.4 10.0 %collective-permute-done = bf16[176,640]{0,1:T(8,128)(2,1)S(1)} collective-permute-done((bf16[176,640]{0,1:T(8,128)(2,1)S(1)}, bf16[176,640]{0,1:T(8,128)(2,1)S(1)}, u32[]{:S(2)}, u32[]{:S(2)}) %collective-permute-start) | collective-permute-done | bytes 225312 | tf_op jit(solution)/shard_map/while/body/eval_jaxpr/ppermute | solution.py:16
  211.8 2.3 multiply_reduce_fusion.21
  217.2 10.0 %collective-permute-done = bf16[176,640]{0,1:T(8,128)(2,1)S(1)} collective-permute-done((bf16[176,640]{0,1:T(8,128)(2,1)S(1)}, bf16[176,640]{0,1:T(8,128)(2,1)S(1)}, u32[]{:S(2)}, u32[]{:S(2)}) %collective-permute-start) | collective-permute-done | bytes 225312 | tf_op jit(solution)/shard_map/while/body/eval_jaxpr/ppermute | solution.py:16
  229.6 2.3 multiply_reduce_fusion.21
  235.1 10.0 %collective-permute-done = bf16[176,640]{0,1:T(8,128)(2,1)S(1)} collective-permute-done((bf16[176,640]{0,1:T(8,128)(2,1)S(1)}, bf16[176,640]{0,1:T(8,128)(2,1)S(1)}, u32[]{:S(2)}, u32[]{:S(2)}) %collective-permute-start) | collective-permute-done | bytes 225312 | tf_op jit(solution)/shard_map/while/body/eval_jaxpr/ppermute | solution.py:16
  247.4 2.3 multiply_reduce_fusion.21
  252.9 10.0 %collective-permute-done = bf16[176,640]{0,1:T(8,128)(2,1)S(1)} collective-permute-done((bf16[176,640]{0,1:T(8,128)(2,1)S(1)}, bf16[176,640]{0,1:T(8,128)(2,1)S(1)}, u32[]{:S(2)}, u32[]{:S(2)}) %collective-permute-start) | collective-permute-done | bytes 225312 | tf_op jit(solution)/shard_map/while/body/eval_jaxpr/ppermute | solution.py:16
  265.3 2.3 multiply_reduce_fusion.21
  270.7 10.0 %collective-permute-done = bf16[176,640]{0,1:T(8,128)(2,1)S(1)} collective-permute-done((bf16[176,640]{0,1:T(8,128)(2,1)S(1)}, bf16[176,640]{0,1:T(8,128)(2,1)S(1)}, u32[]{:S(2)}, u32[]{:S(2)}) %collective-permute-start) | collective-permute-done | bytes 225312 | tf_op jit(solution)/shard_map/while/body/eval_jaxpr/ppermute | solution.py:16
  283.1 2.3 multiply_reduce_fusion.21
  288.6 10.0 %collective-permute-done = bf16[176,640]{0,1:T(8,128)(2,1)S(1)} collective-permute-done((bf16[176,640]{0,1:T(8,128)(2,1)S(1)}, bf16[176,640]{0,1:T(8,128)(2,1)S(1)}, u32[]{:S(2)}, u32[]{:S(2)}) %collective-permute-start) | collective-permute-done | bytes 225312 | tf_op jit(solution)/shard_map/while/body/eval_jaxpr/ppermute | solution.py:16
  300.9 2.3 multiply_reduce_fusion.21
  306.4 10.0 %collective-permute-done = bf16[176,640]{0,1:T(8,128)(2,1)S(1)} collective-permute-done((bf16[176,640]{0,1:T(8,128)(2,1)S(1)}, bf16[176,640]{0,1:T(8,128)(2,1)S(1)}, u32[]{:S(2)}, u32[]{:S(2)}) %collective-permute-start) | collective-permute-done | bytes 225312 | tf_op jit(solution)/shard_map/while/body/eval_jaxpr/ppermute | solution.py:16
  318.8 2.3 multiply_reduce_fusion.21
  324.3 10.0 %collective-permute-done = bf16[176,640]{0,1:T(8,128)(2,1)S(1)} collective-permute-done((bf16[176,640]{0,1:T(8,128)(2,1)S(1)}, bf16[176,640]{0,1:T(8,128)(2,1)S(1)}, u32[]{:S(2)}, u32[]{:S(2)}) %collective-permute-start) | collective-permute-done | bytes 225312 | tf_op jit(solution)/shard_map/while/body/eval_jaxpr/ppermute | solution.py:16
  336.6 2.3 multiply_reduce_fusion.21
  342.1 10.0 %collective-permute-done = bf16[176,640]{0,1:T(8,128)(2,1)S(1)} collective-permute-done((bf16[176,640]{0,1:T(8,128)(2,1)S(1)}, bf16[176,640]{0,1:T(8,128)(2,1)S(1)}, u32[]{:S(2)}, u32[]{:S(2)}) %collective-permute-start) | collective-permute-done | bytes 225312 | tf_op jit(solution)/shard_map/while/body/eval_jaxpr/ppermute | solution.py:16
  354.4 2.3 multiply_reduce_fusion.21
  (324 shorter events, 100.2 us)
Async XLA Ops:
  85.2 2.3 copy-start.2
  90.4 12.0 %collective-permute-start = (bf16[176,640]{0,1:T(8,128)(2,1)S(1)}, bf16[176,640]{0,1:T(8,128)(2,1)S(1)}, u32[]{:S(2)}, u32[]{:S(2)}) collective-permute-start(bf16[176,640]{0,1:T(8,128)(2,1)S(1)} %get-tuple-element.459), channel_id=1, source_target_pairs={{480,0},{0,32},{32,64},{64,96},{96,128},{128,160},{160,192},{192,2... | collective-permute-start | bytes 675848 | tf_op jit(solution)/shard_map/while/body/eval_jaxpr/ppermute | solution.py:16
  103.7 1.1 copy-start.3
  108.3 12.0 %collective-permute-start = (bf16[176,640]{0,1:T(8,128)(2,1)S(1)}, bf16[176,640]{0,1:T(8,128)(2,1)S(1)}, u32[]{:S(2)}, u32[]{:S(2)}) collective-permute-start(bf16[176,640]{0,1:T(8,128)(2,1)S(1)} %get-tuple-element.459), channel_id=1, source_target_pairs={{480,0},{0,32},{32,64},{64,96},{96,128},{128,160},{160,192},{192,2... | collective-permute-start | bytes 675848 | tf_op jit(solution)/shard_map/while/body/eval_jaxpr/ppermute | solution.py:16
  121.5 1.1 copy-start.3
  126.1 12.0 %collective-permute-start = (bf16[176,640]{0,1:T(8,128)(2,1)S(1)}, bf16[176,640]{0,1:T(8,128)(2,1)S(1)}, u32[]{:S(2)}, u32[]{:S(2)}) collective-permute-start(bf16[176,640]{0,1:T(8,128)(2,1)S(1)} %get-tuple-element.459), channel_id=1, source_target_pairs={{480,0},{0,32},{32,64},{64,96},{96,128},{128,160},{160,192},{192,2... | collective-permute-start | bytes 675848 | tf_op jit(solution)/shard_map/while/body/eval_jaxpr/ppermute | solution.py:16
  139.3 1.1 copy-start.3
  143.9 12.0 %collective-permute-start = (bf16[176,640]{0,1:T(8,128)(2,1)S(1)}, bf16[176,640]{0,1:T(8,128)(2,1)S(1)}, u32[]{:S(2)}, u32[]{:S(2)}) collective-permute-start(bf16[176,640]{0,1:T(8,128)(2,1)S(1)} %get-tuple-element.459), channel_id=1, source_target_pairs={{480,0},{0,32},{32,64},{64,96},{96,128},{128,160},{160,192},{192,2... | collective-permute-start | bytes 675848 | tf_op jit(solution)/shard_map/while/body/eval_jaxpr/ppermute | solution.py:16
  157.2 1.1 copy-start.3
  161.8 12.0 %collective-permute-start = (bf16[176,640]{0,1:T(8,128)(2,1)S(1)}, bf16[176,640]{0,1:T(8,128)(2,1)S(1)}, u32[]{:S(2)}, u32[]{:S(2)}) collective-permute-start(bf16[176,640]{0,1:T(8,128)(2,1)S(1)} %get-tuple-element.459), channel_id=1, source_target_pairs={{480,0},{0,32},{32,64},{64,96},{96,128},{128,160},{160,192},{192,2... | collective-permute-start | bytes 675848 | tf_op jit(solution)/shard_map/while/body/eval_jaxpr/ppermute | solution.py:16
  175.0 1.1 copy-start.3
  179.6 12.0 %collective-permute-start = (bf16[176,640]{0,1:T(8,128)(2,1)S(1)}, bf16[176,640]{0,1:T(8,128)(2,1)S(1)}, u32[]{:S(2)}, u32[]{:S(2)}) collective-permute-start(bf16[176,640]{0,1:T(8,128)(2,1)S(1)} %get-tuple-element.459), channel_id=1, source_target_pairs={{480,0},{0,32},{32,64},{64,96},{96,128},{128,160},{160,192},{192,2... | collective-permute-start | bytes 675848 | tf_op jit(solution)/shard_map/while/body/eval_jaxpr/ppermute | solution.py:16
  192.8 1.1 copy-start.3
  197.4 12.0 %collective-permute-start = (bf16[176,640]{0,1:T(8,128)(2,1)S(1)}, bf16[176,640]{0,1:T(8,128)(2,1)S(1)}, u32[]{:S(2)}, u32[]{:S(2)}) collective-permute-start(bf16[176,640]{0,1:T(8,128)(2,1)S(1)} %get-tuple-element.459), channel_id=1, source_target_pairs={{480,0},{0,32},{32,64},{64,96},{96,128},{128,160},{160,192},{192,2... | collective-permute-start | bytes 675848 | tf_op jit(solution)/shard_map/while/body/eval_jaxpr/ppermute | solution.py:16
  210.7 1.1 copy-start.3
  215.3 12.0 %collective-permute-start = (bf16[176,640]{0,1:T(8,128)(2,1)S(1)}, bf16[176,640]{0,1:T(8,128)(2,1)S(1)}, u32[]{:S(2)}, u32[]{:S(2)}) collective-permute-start(bf16[176,640]{0,1:T(8,128)(2,1)S(1)} %get-tuple-element.459), channel_id=1, source_target_pairs={{480,0},{0,32},{32,64},{64,96},{96,128},{128,160},{160,192},{192,2... | collective-permute-start | bytes 675848 | tf_op jit(solution)/shard_map/while/body/eval_jaxpr/ppermute | solution.py:16
  228.5 1.1 copy-start.3
  233.1 12.0 %collective-permute-start = (bf16[176,640]{0,1:T(8,128)(2,1)S(1)}, bf16[176,640]{0,1:T(8,128)(2,1)S(1)}, u32[]{:S(2)}, u32[]{:S(2)}) collective-permute-start(bf16[176,640]{0,1:T(8,128)(2,1)S(1)} %get-tuple-element.459), channel_id=1, source_target_pairs={{480,0},{0,32},{32,64},{64,96},{96,128},{128,160},{160,192},{192,2... | collective-permute-start | bytes 675848 | tf_op jit(solution)/shard_map/while/body/eval_jaxpr/ppermute | solution.py:16
  246.3 1.1 copy-start.3
  250.9 12.0 %collective-permute-start = (bf16[176,640]{0,1:T(8,128)(2,1)S(1)}, bf16[176,640]{0,1:T(8,128)(2,1)S(1)}, u32[]{:S(2)}, u32[]{:S(2)}) collective-permute-start(bf16[176,640]{0,1:T(8,128)(2,1)S(1)} %get-tuple-element.459), channel_id=1, source_target_pairs={{480,0},{0,32},{32,64},{64,96},{96,128},{128,160},{160,192},{192,2... | collective-permute-start | bytes 675848 | tf_op jit(solution)/shard_map/while/body/eval_jaxpr/ppermute | solution.py:16
  264.2 1.1 copy-start.3
  268.8 12.0 %collective-permute-start = (bf16[176,640]{0,1:T(8,128)(2,1)S(1)}, bf16[176,640]{0,1:T(8,128)(2,1)S(1)}, u32[]{:S(2)}, u32[]{:S(2)}) collective-permute-start(bf16[176,640]{0,1:T(8,128)(2,1)S(1)} %get-tuple-element.459), channel_id=1, source_target_pairs={{480,0},{0,32},{32,64},{64,96},{96,128},{128,160},{160,192},{192,2... | collective-permute-start | bytes 675848 | tf_op jit(solution)/shard_map/while/body/eval_jaxpr/ppermute | solution.py:16
  282.0 1.1 copy-start.3
  286.6 12.0 %collective-permute-start = (bf16[176,640]{0,1:T(8,128)(2,1)S(1)}, bf16[176,640]{0,1:T(8,128)(2,1)S(1)}, u32[]{:S(2)}, u32[]{:S(2)}) collective-permute-start(bf16[176,640]{0,1:T(8,128)(2,1)S(1)} %get-tuple-element.459), channel_id=1, source_target_pairs={{480,0},{0,32},{32,64},{64,96},{96,128},{128,160},{160,192},{192,2... | collective-permute-start | bytes 675848 | tf_op jit(solution)/shard_map/while/body/eval_jaxpr/ppermute | solution.py:16
  299.8 1.1 copy-start.3
  304.4 12.0 %collective-permute-start = (bf16[176,640]{0,1:T(8,128)(2,1)S(1)}, bf16[176,640]{0,1:T(8,128)(2,1)S(1)}, u32[]{:S(2)}, u32[]{:S(2)}) collective-permute-start(bf16[176,640]{0,1:T(8,128)(2,1)S(1)} %get-tuple-element.459), channel_id=1, source_target_pairs={{480,0},{0,32},{32,64},{64,96},{96,128},{128,160},{160,192},{192,2... | collective-permute-start | bytes 675848 | tf_op jit(solution)/shard_map/while/body/eval_jaxpr/ppermute | solution.py:16
  317.7 1.1 copy-start.3
  322.3 12.0 %collective-permute-start = (bf16[176,640]{0,1:T(8,128)(2,1)S(1)}, bf16[176,640]{0,1:T(8,128)(2,1)S(1)}, u32[]{:S(2)}, u32[]{:S(2)}) collective-permute-start(bf16[176,640]{0,1:T(8,128)(2,1)S(1)} %get-tuple-element.459), channel_id=1, source_target_pairs={{480,0},{0,32},{32,64},{64,96},{96,128},{128,160},{160,192},{192,2... | collective-permute-start | bytes 675848 | tf_op jit(solution)/shard_map/while/body/eval_jaxpr/ppermute | solution.py:16
  335.5 1.1 copy-start.3
  340.1 12.0 %collective-permute-start = (bf16[176,640]{0,1:T(8,128)(2,1)S(1)}, bf16[176,640]{0,1:T(8,128)(2,1)S(1)}, u32[]{:S(2)}, u32[]{:S(2)}) collective-permute-start(bf16[176,640]{0,1:T(8,128)(2,1)S(1)} %get-tuple-element.459), channel_id=1, source_target_pairs={{480,0},{0,32},{32,64},{64,96},{96,128},{128,160},{160,192},{192,2... | collective-permute-start | bytes 675848 | tf_op jit(solution)/shard_map/while/body/eval_jaxpr/ppermute | solution.py:16
  353.3 1.1 copy-start.3
  358.0 1.1 copy-start.1
  (2 other events, 1.9 us)
where the time goes:
time: 361 us; the launch traced here: 359 us
  waiting for transfers between devices  151 us (42%)
  blocking collectives  70.2 us (19%)
  other arithmetic  48.3 us (13%)
  matrix products  44.4 us (12%)
  starting transfers between devices  28.8 us (8%)
  local copies, waits for them, and re-layouts  13.3 us (4%)
    ppermute x15, waiting for transfers between devices, shifted(): return lax.ppermute(block, axis, route)  151 us
    all_gather x1, blocking collectives, body(): panel_rows = lax.all_gather(own_seeds, 'wide', axis=0, tiled=True)  70.2 us
    dot_general x16, matrix products, compare(): jnp.einsum('tnw,snw->nts', target_windows, seed_window, preferred_element...  36.8 us
    ppermute x15, starting transfers between devices, shifted(): return lax.ppermute(block, axis, route)  28.8 us
    dynamic_update_slice x15, other arithmetic, record(): lax.dynamic_update_index_in_dim(results[0], dispersion, source, 0)  10.2 us
    div x17, other arithmetic, prepare(): mean_all = jnp.sum(values * weight, axis=1) / total_valid  9.57 us
    reduce_sum x17, other arithmetic, prepare(): spread = jnp.sum(centred * centred, axis=2)  8.51 us
    dot_general x16, matrix products, compare(): jnp.einsum('tf,sf->ts', target_whole, seed_whole, preferred_element_type=...  7.54 us
  transfers between devices with their start and end apart: 15, of which 15 were waited for; matrix products, arithmetic and copies ran while one was open for 0% of the time, Pallas kernels for 0%

commit v1 on v0

--- a/solution.py
+++ b/solution.py
@@ -63,7 +63,9 @@
     total_valid = jnp.sum(scrub_mask.astype(jnp.float32))
     target_windows, target_whole = prepare(series, scrub_mask)
     blocks = lax.axis_size("blk")
-    panel_rows = lax.all_gather(own_seeds, "wide", axis=0, tiled=True)
+    panel_rows = jnp.concatenate(
+        lax.all_to_all(jnp.stack([own_seeds] * lax.axis_size("wide")), "wide", 0, 0), axis=0
+    )
     seed_window, seed_whole = prepare(panel_rows, scrub_mask)
     panel_size = panel_rows.shape[0]
     own_block = lax.axis_index("blk")

time: 361 us -> 323 us (0.89)
  blocking collectives: 70.2 us -> 0 us
  waiting for transfers between devices: 151 us -> 167 us
  starting transfers between devices: 28.8 us -> 44.7 us
  matrix products: 44.4 us -> 54.7 us
  other arithmetic: 48.3 us -> 38.6 us
    all_gather x1 -> x0, blocking collectives: 70.2 us -> none  [body(): panel_rows = lax.all_gather(own_seeds, 'wide', axis=0, tiled=True)]
    all_to_all x0 -> x1, waiting for transfers between devices: none -> 16.3 us  [body(): lax.all_to_all(jnp.stack([own_seeds] * lax.axis_size('wide')), 'wide', 0, 0)]
    all_to_all x0 -> x1, starting transfers between devices: none -> 16.1 us  [body(): lax.all_to_all(jnp.stack([own_seeds] * lax.axis_size('wide')), 'wide', 0, 0)]
    dot_general x16, matrix products: 7.54 us -> 17.7 us  [compare(): jnp.einsum('tf,sf->ts', target_whole, seed_whole, preferred_element_type=...]
    dynamic_update_slice x15, other arithmetic: 10.2 us -> 0.62 us  [record(): lax.dynamic_update_index_in_dim(results[0], dispersion, source, 0)]
  transfers between devices with their start and end apart: 15 -> 16, of which waited for: 15 -> 16; matrix products, arithmetic and copies ran while one was open for 0% -> 2% of each run, Pallas kernels for 0% -> 0%
where the time goes in v1:
time: 323 us; the launch traced here: 322 us
  waiting for transfers between devices  167 us (52%)
  matrix products  54.7 us (17%)
  starting transfers between devices  44.7 us (14%)
  other arithmetic  38.6 us (12%)
  local copies, waits for them, and re-layouts  13.3 us (4%)
    ppermute x15, waiting for transfers between devices, shifted(): return lax.ppermute(block, axis, route)  151 us
    dot_general x16, matrix products, compare(): jnp.einsum('tnw,snw->nts', target_windows, seed_window, preferred_element...  37 us
    ppermute x15, starting transfers between devices, shifted(): return lax.ppermute(block, axis, route)  28.6 us
    dot_general x16, matrix products, compare(): jnp.einsum('tf,sf->ts', target_whole, seed_whole, preferred_element_type=...  17.7 us
    all_to_all x1, waiting for transfers between devices, body(): lax.all_to_all(jnp.stack([own_seeds] * lax.axis_size('wide')), 'wide', 0, 0)  16.3 us
    all_to_all x1, starting transfers between devices, body(): lax.all_to_all(jnp.stack([own_seeds] * lax.axis_size('wide')), 'wide', 0, 0)  16.1 us
    div x17, other arithmetic, prepare(): mean_all = jnp.sum(values * weight, axis=1) / total_valid  9.57 us
    reduce_sum x17, other arithmetic, prepare(): spread = jnp.sum(centred * centred, axis=2)  8.62 us
  transfers between devices with their start and end apart: 16, of which 16 were waited for; matrix products, arithmetic and copies ran while one was open for 2% of the time, Pallas kernels for 0%

profile of v1, /device:TPU:4, one launch (start us, length us, event | category | flops | bytes accessed | tf_op | source)
XLA Modules:
  0.0 321.9 jit_solution(12156885371657415044)
XLA Ops:
  3.7 16.1 %all-to-all-start = ((bf16[32,8,640]{2,1,0:T(8,128)(2,1)}), bf16[32,8,640]{2,1,0:T(8,128)(2,1)S(1)}, u32[]{:S(2)}, u32[]{:S(2)}) async-start(bf16[32,8,640]{2,1,0:T(8,128)(2,1)} %stack.2), calls=%async_computation | async-start | bytes 655360 | tf_op jit(solution)/shard_map/all_to_all | solution.py:67
  28.3 16.3 %all-to-all-done = bf16[32,8,640]{2,1,0:T(8,128)(2,1)S(1)} async-done(((bf16[32,8,640]{2,1,0:T(8,128)(2,1)}), bf16[32,8,640]{2,1,0:T(8,128)(2,1)S(1)}, u32[]{:S(2)}, u32[]{:S(2)}) %all-to-all-start) | async-done | bytes 327712 | tf_op jit(solution)/shard_map/all_to_all | solution.py:67
  49.1 2.3 multiply_reduce_fusion.5
  54.5 266.3 %while.20 = (s32[]{:T(128)}, bf16[16,176,256]{2,1,0:T(8,128)(2,1)S(1)}, bf16[16,176,256]{2,1,0:T(8,128)(2,1)}, bf16[176,640]{0,1:T(8,128)(2,1)S(1)}, f32[20,60]{...) while((s32[]{:T(128)}, ...), condition=%wide.region_20.21_spmd, body=%wide.region_13.20_spmd.sunk | while | flops 177675536 | bytes 21564408 | solution.py:98
  56.5 10.0 %collective-permute-done = bf16[176,640]{0,1:T(8,128)(2,1)S(1)} collective-permute-done((bf16[176,640]{0,1:T(8,128)(2,1)S(1)}, bf16[176,640]{0,1:T(8,128)(2,1)S(1)}, u32[]{:S(2)}, u32[]{:S(2)}) %collective-permute-start) | collective-permute-done | bytes 225312 | tf_op jit(solution)/shard_map/while/body/eval_jaxpr/ppermute | solution.py:16
  74.2 10.0 %collective-permute-done = bf16[176,640]{0,1:T(8,128)(2,1)S(1)} collective-permute-done((bf16[176,640]{0,1:T(8,128)(2,1)S(1)}, bf16[176,640]{0,1:T(8,128)(2,1)S(1)}, u32[]{:S(2)}, u32[]{:S(2)}) %collective-permute-start) | collective-permute-done | bytes 225312 | tf_op jit(solution)/shard_map/while/body/eval_jaxpr/ppermute | solution.py:16
  92.0 10.0 %collective-permute-done = bf16[176,640]{0,1:T(8,128)(2,1)S(1)} collective-permute-done((bf16[176,640]{0,1:T(8,128)(2,1)S(1)}, bf16[176,640]{0,1:T(8,128)(2,1)S(1)}, u32[]{:S(2)}, u32[]{:S(2)}) %collective-permute-start) | collective-permute-done | bytes 225312 | tf_op jit(solution)/shard_map/while/body/eval_jaxpr/ppermute | solution.py:16
  104.3 2.3 multiply_reduce_fusion.19
  109.7 10.0 %collective-permute-done = bf16[176,640]{0,1:T(8,128)(2,1)S(1)} collective-permute-done((bf16[176,640]{0,1:T(8,128)(2,1)S(1)}, bf16[176,640]{0,1:T(8,128)(2,1)S(1)}, u32[]{:S(2)}, u32[]{:S(2)}) %collective-permute-start) | collective-permute-done | bytes 225312 | tf_op jit(solution)/shard_map/while/body/eval_jaxpr/ppermute | solution.py:16
  122.0 2.3 multiply_reduce_fusion.19
  127.5 10.0 %collective-permute-done = bf16[176,640]{0,1:T(8,128)(2,1)S(1)} collective-permute-done((bf16[176,640]{0,1:T(8,128)(2,1)S(1)}, bf16[176,640]{0,1:T(8,128)(2,1)S(1)}, u32[]{:S(2)}, u32[]{:S(2)}) %collective-permute-start) | collective-permute-done | bytes 225312 | tf_op jit(solution)/shard_map/while/body/eval_jaxpr/ppermute | solution.py:16
  139.8 2.3 multiply_reduce_fusion.19
  145.2 10.0 %collective-permute-done = bf16[176,640]{0,1:T(8,128)(2,1)S(1)} collective-permute-done((bf16[176,640]{0,1:T(8,128)(2,1)S(1)}, bf16[176,640]{0,1:T(8,128)(2,1)S(1)}, u32[]{:S(2)}, u32[]{:S(2)}) %collective-permute-start) | collective-permute-done | bytes 225312 | tf_op jit(solution)/shard_map/while/body/eval_jaxpr/ppermute | solution.py:16
  157.5 2.3 multiply_reduce_fusion.19
  163.0 10.0 %collective-permute-done = bf16[176,640]{0,1:T(8,128)(2,1)S(1)} collective-permute-done((bf16[176,640]{0,1:T(8,128)(2,1)S(1)}, bf16[176,640]{0,1:T(8,128)(2,1)S(1)}, u32[]{:S(2)}, u32[]{:S(2)}) %collective-permute-start) | collective-permute-done | bytes 225312 | tf_op jit(solution)/shard_map/while/body/eval_jaxpr/ppermute | solution.py:16
  175.3 2.3 multiply_reduce_fusion.19
  180.8 10.0 %collective-permute-done = bf16[176,640]{0,1:T(8,128)(2,1)S(1)} collective-permute-done((bf16[176,640]{0,1:T(8,128)(2,1)S(1)}, bf16[176,640]{0,1:T(8,128)(2,1)S(1)}, u32[]{:S(2)}, u32[]{:S(2)}) %collective-permute-start) | collective-permute-done | bytes 225312 | tf_op jit(solution)/shard_map/while/body/eval_jaxpr/ppermute | solution.py:16
  193.0 2.3 multiply_reduce_fusion.19
  198.5 10.0 %collective-permute-done = bf16[176,640]{0,1:T(8,128)(2,1)S(1)} collective-permute-done((bf16[176,640]{0,1:T(8,128)(2,1)S(1)}, bf16[176,640]{0,1:T(8,128)(2,1)S(1)}, u32[]{:S(2)}, u32[]{:S(2)}) %collective-permute-start) | collective-permute-done | bytes 225312 | tf_op jit(solution)/shard_map/while/body/eval_jaxpr/ppermute | solution.py:16
  210.8 2.3 multiply_reduce_fusion.19
  216.3 10.0 %collective-permute-done = bf16[176,640]{0,1:T(8,128)(2,1)S(1)} collective-permute-done((bf16[176,640]{0,1:T(8,128)(2,1)S(1)}, bf16[176,640]{0,1:T(8,128)(2,1)S(1)}, u32[]{:S(2)}, u32[]{:S(2)}) %collective-permute-start) | collective-permute-done | bytes 225312 | tf_op jit(solution)/shard_map/while/body/eval_jaxpr/ppermute | solution.py:16
  228.5 2.3 multiply_reduce_fusion.19
  234.0 10.0 %collective-permute-done = bf16[176,640]{0,1:T(8,128)(2,1)S(1)} collective-permute-done((bf16[176,640]{0,1:T(8,128)(2,1)S(1)}, bf16[176,640]{0,1:T(8,128)(2,1)S(1)}, u32[]{:S(2)}, u32[]{:S(2)}) %collective-permute-start) | collective-permute-done | bytes 225312 | tf_op jit(solution)/shard_map/while/body/eval_jaxpr/ppermute | solution.py:16
  246.3 2.3 multiply_reduce_fusion.19
  251.8 10.0 %collective-permute-done = bf16[176,640]{0,1:T(8,128)(2,1)S(1)} collective-permute-done((bf16[176,640]{0,1:T(8,128)(2,1)S(1)}, bf16[176,640]{0,1:T(8,128)(2,1)S(1)}, u32[]{:S(2)}, u32[]{:S(2)}) %collective-permute-start) | collective-permute-done | bytes 225312 | tf_op jit(solution)/shard_map/while/body/eval_jaxpr/ppermute | solution.py:16
  264.0 2.3 multiply_reduce_fusion.19
  269.5 10.0 %collective-permute-done = bf16[176,640]{0,1:T(8,128)(2,1)S(1)} collective-permute-done((bf16[176,640]{0,1:T(8,128)(2,1)S(1)}, bf16[176,640]{0,1:T(8,128)(2,1)S(1)}, u32[]{:S(2)}, u32[]{:S(2)}) %collective-permute-start) | collective-permute-done | bytes 225312 | tf_op jit(solution)/shard_map/while/body/eval_jaxpr/ppermute | solution.py:16
  281.8 2.3 multiply_reduce_fusion.19
  287.3 10.0 %collective-permute-done = bf16[176,640]{0,1:T(8,128)(2,1)S(1)} collective-permute-done((bf16[176,640]{0,1:T(8,128)(2,1)S(1)}, bf16[176,640]{0,1:T(8,128)(2,1)S(1)}, u32[]{:S(2)}, u32[]{:S(2)}) %collective-permute-start) | collective-permute-done | bytes 225312 | tf_op jit(solution)/shard_map/while/body/eval_jaxpr/ppermute | solution.py:16
  299.5 2.3 multiply_reduce_fusion.19
  305.0 10.0 %collective-permute-done = bf16[176,640]{0,1:T(8,128)(2,1)S(1)} collective-permute-done((bf16[176,640]{0,1:T(8,128)(2,1)S(1)}, bf16[176,640]{0,1:T(8,128)(2,1)S(1)}, u32[]{:S(2)}, u32[]{:S(2)}) %collective-permute-start) | collective-permute-done | bytes 225312 | tf_op jit(solution)/shard_map/while/body/eval_jaxpr/ppermute | solution.py:16
  317.3 2.3 multiply_reduce_fusion.19
  (374 shorter events, 102.8 us)
Async XLA Ops:
  0.6 22.9 %copy-start = (bf16[176,640]{1,0:T(8,128)(2,1)S(1)}, bf16[176,640]{1,0:T(8,128)(2,1)}, u32[]{:S(2)}) copy-start(bf16[176,640]{1,0:T(8,128)(2,1)} %param.5) | copy-start | bytes 675844
  3.7 40.9 %all-to-all-start = ((bf16[32,8,640]{2,1,0:T(8,128)(2,1)}), bf16[32,8,640]{2,1,0:T(8,128)(2,1)S(1)}, u32[]{:S(2)}, u32[]{:S(2)}) async-start(bf16[32,8,640]{2,1,0:T(8,128)(2,1)} %stack.2), calls=%async_computation | async-start | bytes 655360 | tf_op jit(solution)/shard_map/all_to_all | solution.py:67
  26.0 21.8 %copy-start.6 = (f32[20]{0:T(128)}, f32[20]{0:T(128)S(1)}, u32[]{:S(2)}) copy-start(f32[20]{0:T(128)S(1)} %reduce_sum.264) | copy-start | bytes 244
  26.6 18.0 %copy-start.4 = (f32[176,20]{0,1:T(8,128)}, f32[176,20]{0,1:T(8,128)S(1)}, u32[]{:S(2)}) copy-start(f32[176,20]{0,1:T(8,128)S(1)} %broadcast_divide_fusion.3) | copy-start | bytes 42244
  54.5 12.9 %copy-start.1 = (bf16[16,176,256]{2,1,0:T(8,128)(2,1)}, bf16[16,176,256]{2,1,0:T(8,128)(2,1)S(1)}, u32[]{:S(2)}) copy-start(bf16[16,176,256]{2,1,0:T(8,128)(2,1)S(1)} %get-tuple-element.457) | copy-start | bytes 4325380 | tf_op jit(solution)/shard_map/while
  54.5 12.0 %collective-permute-start = (bf16[176,640]{0,1:T(8,128)(2,1)S(1)}, bf16[176,640]{0,1:T(8,128)(2,1)S(1)}, u32[]{:S(2)}, u32[]{:S(2)}) collective-permute-start(bf16[176,640]{0,1:T(8,128)(2,1)S(1)} %get-tuple-element.459), channel_id=1, source_target_pairs={{480,0},{0,32},{32,64},{64,96},{96,128},{128,160},{160,192},{192,2... | collective-permute-start | bytes 675848 | tf_op jit(solution)/shard_map/while/body/eval_jaxpr/ppermute | solution.py:16
  72.3 12.9 %copy-start.1 = (bf16[16,176,256]{2,1,0:T(8,128)(2,1)}, bf16[16,176,256]{2,1,0:T(8,128)(2,1)S(1)}, u32[]{:S(2)}) copy-start(bf16[16,176,256]{2,1,0:T(8,128)(2,1)S(1)} %get-tuple-element.457) | copy-start | bytes 4325380 | tf_op jit(solution)/shard_map/while
  72.3 12.0 %collective-permute-start = (bf16[176,640]{0,1:T(8,128)(2,1)S(1)}, bf16[176,640]{0,1:T(8,128)(2,1)S(1)}, u32[]{:S(2)}, u32[]{:S(2)}) collective-permute-start(bf16[176,640]{0,1:T(8,128)(2,1)S(1)} %get-tuple-element.459), channel_id=1, source_target_pairs={{480,0},{0,32},{32,64},{64,96},{96,128},{128,160},{160,192},{192,2... | collective-permute-start | bytes 675848 | tf_op jit(solution)/shard_map/while/body/eval_jaxpr/ppermute | solution.py:16
  90.0 12.9 %copy-start.1 = (bf16[16,176,256]{2,1,0:T(8,128)(2,1)}, bf16[16,176,256]{2,1,0:T(8,128)(2,1)S(1)}, u32[]{:S(2)}) copy-start(bf16[16,176,256]{2,1,0:T(8,128)(2,1)S(1)} %get-tuple-element.457) | copy-start | bytes 4325380 | tf_op jit(solution)/shard_map/while
  90.0 12.0 %collective-permute-start = (bf16[176,640]{0,1:T(8,128)(2,1)S(1)}, bf16[176,640]{0,1:T(8,128)(2,1)S(1)}, u32[]{:S(2)}, u32[]{:S(2)}) collective-permute-start(bf16[176,640]{0,1:T(8,128)(2,1)S(1)} %get-tuple-element.459), channel_id=1, source_target_pairs={{480,0},{0,32},{32,64},{64,96},{96,128},{128,160},{160,192},{192,2... | collective-permute-start | bytes 675848 | tf_op jit(solution)/shard_map/while/body/eval_jaxpr/ppermute | solution.py:16
  107.8 12.9 %copy-start.1 = (bf16[16,176,256]{2,1,0:T(8,128)(2,1)}, bf16[16,176,256]{2,1,0:T(8,128)(2,1)S(1)}, u32[]{:S(2)}) copy-start(bf16[16,176,256]{2,1,0:T(8,128)(2,1)S(1)} %get-tuple-element.457) | copy-start | bytes 4325380 | tf_op jit(solution)/shard_map/while
  107.8 12.0 %collective-permute-start = (bf16[176,640]{0,1:T(8,128)(2,1)S(1)}, bf16[176,640]{0,1:T(8,128)(2,1)S(1)}, u32[]{:S(2)}, u32[]{:S(2)}) collective-permute-start(bf16[176,640]{0,1:T(8,128)(2,1)S(1)} %get-tuple-element.459), channel_id=1, source_target_pairs={{480,0},{0,32},{32,64},{64,96},{96,128},{128,160},{160,192},{192,2... | collective-permute-start | bytes 675848 | tf_op jit(solution)/shard_map/while/body/eval_jaxpr/ppermute | solution.py:16
  125.5 12.9 %copy-start.1 = (bf16[16,176,256]{2,1,0:T(8,128)(2,1)}, bf16[16,176,256]{2,1,0:T(8,128)(2,1)S(1)}, u32[]{:S(2)}) copy-start(bf16[16,176,256]{2,1,0:T(8,128)(2,1)S(1)} %get-tuple-element.457) | copy-start | bytes 4325380 | tf_op jit(solution)/shard_map/while
  125.5 12.0 %collective-permute-start = (bf16[176,640]{0,1:T(8,128)(2,1)S(1)}, bf16[176,640]{0,1:T(8,128)(2,1)S(1)}, u32[]{:S(2)}, u32[]{:S(2)}) collective-permute-start(bf16[176,640]{0,1:T(8,128)(2,1)S(1)} %get-tuple-element.459), channel_id=1, source_target_pairs={{480,0},{0,32},{32,64},{64,96},{96,128},{128,160},{160,192},{192,2... | collective-permute-start | bytes 675848 | tf_op jit(solution)/shard_map/while/body/eval_jaxpr/ppermute | solution.py:16
  143.3 12.9 %copy-start.1 = (bf16[16,176,256]{2,1,0:T(8,128)(2,1)}, bf16[16,176,256]{2,1,0:T(8,128)(2,1)S(1)}, u32[]{:S(2)}) copy-start(bf16[16,176,256]{2,1,0:T(8,128)(2,1)S(1)} %get-tuple-element.457) | copy-start | bytes 4325380 | tf_op jit(solution)/shard_map/while
  143.3 12.0 %collective-permute-start = (bf16[176,640]{0,1:T(8,128)(2,1)S(1)}, bf16[176,640]{0,1:T(8,128)(2,1)S(1)}, u32[]{:S(2)}, u32[]{:S(2)}) collective-permute-start(bf16[176,640]{0,1:T(8,128)(2,1)S(1)} %get-tuple-element.459), channel_id=1, source_target_pairs={{480,0},{0,32},{32,64},{64,96},{96,128},{128,160},{160,192},{192,2... | collective-permute-start | bytes 675848 | tf_op jit(solution)/shard_map/while/body/eval_jaxpr/ppermute | solution.py:16
  161.0 12.9 %copy-start.1 = (bf16[16,176,256]{2,1,0:T(8,128)(2,1)}, bf16[16,176,256]{2,1,0:T(8,128)(2,1)S(1)}, u32[]{:S(2)}) copy-start(bf16[16,176,256]{2,1,0:T(8,128)(2,1)S(1)} %get-tuple-element.457) | copy-start | bytes 4325380 | tf_op jit(solution)/shard_map/while
  161.0 12.0 %collective-permute-start = (bf16[176,640]{0,1:T(8,128)(2,1)S(1)}, bf16[176,640]{0,1:T(8,128)(2,1)S(1)}, u32[]{:S(2)}, u32[]{:S(2)}) collective-permute-start(bf16[176,640]{0,1:T(8,128)(2,1)S(1)} %get-tuple-element.459), channel_id=1, source_target_pairs={{480,0},{0,32},{32,64},{64,96},{96,128},{128,160},{160,192},{192,2... | collective-permute-start | bytes 675848 | tf_op jit(solution)/shard_map/while/body/eval_jaxpr/ppermute | solution.py:16
  178.8 12.9 %copy-start.1 = (bf16[16,176,256]{2,1,0:T(8,128)(2,1)}, bf16[16,176,256]{2,1,0:T(8,128)(2,1)S(1)}, u32[]{:S(2)}) copy-start(bf16[16,176,256]{2,1,0:T(8,128)(2,1)S(1)} %get-tuple-element.457) | copy-start | bytes 4325380 | tf_op jit(solution)/shard_map/while
  178.8 12.0 %collective-permute-start = (bf16[176,640]{0,1:T(8,128)(2,1)S(1)}, bf16[176,640]{0,1:T(8,128)(2,1)S(1)}, u32[]{:S(2)}, u32[]{:S(2)}) collective-permute-start(bf16[176,640]{0,1:T(8,128)(2,1)S(1)} %get-tuple-element.459), channel_id=1, source_target_pairs={{480,0},{0,32},{32,64},{64,96},{96,128},{128,160},{160,192},{192,2... | collective-permute-start | bytes 675848 | tf_op jit(solution)/shard_map/while/body/eval_jaxpr/ppermute | solution.py:16
  196.5 12.0 %collective-permute-start = (bf16[176,640]{0,1:T(8,128)(2,1)S(1)}, bf16[176,640]{0,1:T(8,128)(2,1)S(1)}, u32[]{:S(2)}, u32[]{:S(2)}) collective-permute-start(bf16[176,640]{0,1:T(8,128)(2,1)S(1)} %get-tuple-element.459), channel_id=1, source_target_pairs={{480,0},{0,32},{32,64},{64,96},{96,128},{128,160},{160,192},{192,2... | collective-permute-start | bytes 675848 | tf_op jit(solution)/shard_map/while/body/eval_jaxpr/ppermute | solution.py:16
  214.3 12.0 %collective-permute-start = (bf16[176,640]{0,1:T(8,128)(2,1)S(1)}, bf16[176,640]{0,1:T(8,128)(2,1)S(1)}, u32[]{:S(2)}, u32[]{:S(2)}) collective-permute-start(bf16[176,640]{0,1:T(8,128)(2,1)S(1)} %get-tuple-element.459), channel_id=1, source_target_pairs={{480,0},{0,32},{32,64},{64,96},{96,128},{128,160},{160,192},{192,2... | collective-permute-start | bytes 675848 | tf_op jit(solution)/shard_map/while/body/eval_jaxpr/ppermute | solution.py:16
  232.0 12.9 %copy-start.1 = (bf16[16,176,256]{2,1,0:T(8,128)(2,1)}, bf16[16,176,256]{2,1,0:T(8,128)(2,1)S(1)}, u32[]{:S(2)}) copy-start(bf16[16,176,256]{2,1,0:T(8,128)(2,1)S(1)} %get-tuple-element.457) | copy-start | bytes 4325380 | tf_op jit(solution)/shard_map/while
  232.0 12.0 %collective-permute-start = (bf16[176,640]{0,1:T(8,128)(2,1)S(1)}, bf16[176,640]{0,1:T(8,128)(2,1)S(1)}, u32[]{:S(2)}, u32[]{:S(2)}) collective-permute-start(bf16[176,640]{0,1:T(8,128)(2,1)S(1)} %get-tuple-element.459), channel_id=1, source_target_pairs={{480,0},{0,32},{32,64},{64,96},{96,128},{128,160},{160,192},{192,2... | collective-permute-start | bytes 675848 | tf_op jit(solution)/shard_map/while/body/eval_jaxpr/ppermute | solution.py:16
  249.8 12.9 %copy-start.1 = (bf16[16,176,256]{2,1,0:T(8,128)(2,1)}, bf16[16,176,256]{2,1,0:T(8,128)(2,1)S(1)}, u32[]{:S(2)}) copy-start(bf16[16,176,256]{2,1,0:T(8,128)(2,1)S(1)} %get-tuple-element.457) | copy-start | bytes 4325380 | tf_op jit(solution)/shard_map/while
  249.8 12.0 %collective-permute-start = (bf16[176,640]{0,1:T(8,128)(2,1)S(1)}, bf16[176,640]{0,1:T(8,128)(2,1)S(1)}, u32[]{:S(2)}, u32[]{:S(2)}) collective-permute-start(bf16[176,640]{0,1:T(8,128)(2,1)S(1)} %get-tuple-element.459), channel_id=1, source_target_pairs={{480,0},{0,32},{32,64},{64,96},{96,128},{128,160},{160,192},{192,2... | collective-permute-start | bytes 675848 | tf_op jit(solution)/shard_map/while/body/eval_jaxpr/ppermute | solution.py:16
  267.5 12.9 %copy-start.1 = (bf16[16,176,256]{2,1,0:T(8,128)(2,1)}, bf16[16,176,256]{2,1,0:T(8,128)(2,1)S(1)}, u32[]{:S(2)}) copy-start(bf16[16,176,256]{2,1,0:T(8,128)(2,1)S(1)} %get-tuple-element.457) | copy-start | bytes 4325380 | tf_op jit(solution)/shard_map/while
  267.5 12.0 %collective-permute-start = (bf16[176,640]{0,1:T(8,128)(2,1)S(1)}, bf16[176,640]{0,1:T(8,128)(2,1)S(1)}, u32[]{:S(2)}, u32[]{:S(2)}) collective-permute-start(bf16[176,640]{0,1:T(8,128)(2,1)S(1)} %get-tuple-element.459), channel_id=1, source_target_pairs={{480,0},{0,32},{32,64},{64,96},{96,128},{128,160},{160,192},{192,2... | collective-permute-start | bytes 675848 | tf_op jit(solution)/shard_map/while/body/eval_jaxpr/ppermute | solution.py:16
  285.3 12.9 %copy-start.1 = (bf16[16,176,256]{2,1,0:T(8,128)(2,1)}, bf16[16,176,256]{2,1,0:T(8,128)(2,1)S(1)}, u32[]{:S(2)}) copy-start(bf16[16,176,256]{2,1,0:T(8,128)(2,1)S(1)} %get-tuple-element.457) | copy-start | bytes 4325380 | tf_op jit(solution)/shard_map/while
  285.3 12.0 %collective-permute-start = (bf16[176,640]{0,1:T(8,128)(2,1)S(1)}, bf16[176,640]{0,1:T(8,128)(2,1)S(1)}, u32[]{:S(2)}, u32[]{:S(2)}) collective-permute-start(bf16[176,640]{0,1:T(8,128)(2,1)S(1)} %get-tuple-element.459), channel_id=1, source_target_pairs={{480,0},{0,32},{32,64},{64,96},{96,128},{128,160},{160,192},{192,2... | collective-permute-start | bytes 675848 | tf_op jit(solution)/shard_map/while/body/eval_jaxpr/ppermute | solution.py:16
  303.1 12.9 %copy-start.1 = (bf16[16,176,256]{2,1,0:T(8,128)(2,1)}, bf16[16,176,256]{2,1,0:T(8,128)(2,1)S(1)}, u32[]{:S(2)}) copy-start(bf16[16,176,256]{2,1,0:T(8,128)(2,1)S(1)} %get-tuple-element.457) | copy-start | bytes 4325380 | tf_op jit(solution)/shard_map/while
  303.1 12.0 %collective-permute-start = (bf16[176,640]{0,1:T(8,128)(2,1)S(1)}, bf16[176,640]{0,1:T(8,128)(2,1)S(1)}, u32[]{:S(2)}, u32[]{:S(2)}) collective-permute-start(bf16[176,640]{0,1:T(8,128)(2,1)S(1)} %get-tuple-element.459), channel_id=1, source_target_pairs={{480,0},{0,32},{32,64},{64,96},{96,128},{128,160},{160,192},{192,2... | collective-permute-start | bytes 675848 | tf_op jit(solution)/shard_map/while/body/eval_jaxpr/ppermute | solution.py:16
  (26 other events, 71.4 us)
